TPU v7x, 128 devices: a whole 4x4x4 slice. The times are simulated.
128 devices in a mesh: dp: 4 (over y_hi, core), head: 4 (over x), ctx: 8 (over z, y_lo).
Axes of the slice: x: 4, y: 4 (y_hi: 2, y_lo: 2; y = y_hi * 2 + y_lo), z: 4, core: 2. Of those that a mesh axis runs over, the one named last changes fastest.
Arguments:
- video: bfloat16 [16, 64, 24576], P('dp', 'head', 'ctx'), parts along dimension 0, may hold values from -6 to 6
- cache: bfloat16 [8, 64, 24576], P('dp', 'head', 'ctx'), parts along dimension 0, may hold values from -6 to 6
- conv_weight: bfloat16 [3, 3, 288, 192], replicated, may hold values from -0.125 to 0.125
- conv_bias: float32 [192], replicated, may hold values from -3 to 3
- down_weight: bfloat16 [768, 192], replicated, may hold values from -0.21875 to 0.21875
- patch_weight: bfloat16 [768, 5120], P(None, ('head', 'ctx')), may hold values from -0.21875 to 0.21875
- step_index: int32 [4], P('dp'), parts along dimension 0, may hold values from 0 to 999
- mod_weight: bfloat16 [256, 10240], P(None, ('head', 'ctx')), may hold values from -1 to 1
- qkv_weight: bfloat16 [5120, 20, 3, 128], P('ctx', 'head'), may hold values from -0.078125 to 0.078125
Outputs:
- attended: bfloat16 [16384, 2560], P(('dp', 'ctx'), 'head'), parts along dimension 0
There are 4 independent parts, one for each index of `dp`. A program takes and returns all parts, laid end to end along the dimension named above; an argument that names none is the same for every part. Nothing has to cross between parts.
All inputs are finite; a program needn't handle non-finite values.
Results may differ from a plain program's by a relative error of at most 0.015.
The roundings to bfloat16 on the way count: a program that leaves them out, or rounds other values in their place, can miss the bound.
Values may be sent and summed in bfloat16 or wider, within the bound.
No kernel may reach another device: no remote copies, remote signals or barrier semaphores. Data moves between devices by JAX's collectives and lax.ppermute only.
A program may use at most 128 MiB of HBM per device.

v0:
```python
import jax
import jax.numpy as jnp
from jax import lax
from jax.sharding import PartitionSpec as P

D = 5120
HDIM = 128
FREQ = 256


def with_halo(cells, sides, width):
    for axis, dim in sides:
        count = lax.axis_size(axis)
        ends = count - 1
        head = lax.slice_in_dim(cells, 0, width, axis=dim)
        tail = lax.slice_in_dim(cells, cells.shape[dim] - width, cells.shape[dim], axis=dim)
        cells = jnp.concatenate(
            [
                lax.ppermute(tail, axis, [(i, (i + 1) % count) for i in range(ends)]),
                cells,
                lax.ppermute(head, axis, [((i + 1) % count, i) for i in range(ends)]),
            ],
            axis=dim,
        )
    return cells


def silu_act(value):
    return value * jax.nn.sigmoid(value)


def shards(
    video,
    cache,
    conv_weight,
    conv_bias,
    down_weight,
    patch_weight,
    step_index,
    mod_weight,
    qkv_weight,
):
    cin = conv_weight.shape[2] // 3
    cmid = conv_weight.shape[3]
    frame_count = video.shape[0]
    tile_rows = video.shape[1]
    tile_cols = video.shape[2] // cin
    frames = jnp.concatenate([cache, video], 0).reshape(frame_count + 2, tile_rows, tile_cols, cin)
    padded = with_halo(frames, (("head", 1), ("ctx", 2)), 1)
    total = jnp.zeros((frame_count, tile_rows, tile_cols, cmid), jnp.float32)
    for time_tap in range(3):
        for row_tap in range(3):
            slab = padded[time_tap : time_tap + frame_count, row_tap : row_tap + tile_rows]
            stacked = jnp.concatenate(
                [slab[:, :, col_tap : col_tap + tile_cols] for col_tap in range(3)], -1
            )
            total = total + jnp.einsum(
                "fyxc,cd->fyxd",
                stacked,
                conv_weight[time_tap, row_tap],
                preferred_element_type=jnp.float32,
            )
    hidden = silu_act(total + conv_bias).astype(jnp.bfloat16)
    stacked = (
        hidden.reshape(frame_count, tile_rows // 2, 2, tile_cols // 2, 2, cmid)
        .transpose(0, 1, 3, 2, 4, 5)
        .reshape(-1, 4 * cmid)
    )
    reduced = silu_act(jnp.dot(stacked, down_weight, preferred_element_type=jnp.float32)).astype(
        jnp.bfloat16
    )
    reduced = reduced.reshape(frame_count, tile_rows // 2, tile_cols // 2, cmid)
    patches = reduced.reshape(frame_count, tile_rows // 4, 2, tile_cols // 4, 2, cmid).transpose(
        0, 1, 3, 2, 4, 5
    )
    patches = patches.reshape(-1, 4 * cmid)
    half = FREQ // 2
    freqs = jnp.exp(-jnp.log(10000.0) * jnp.arange(half, dtype=jnp.float32) / half)
    angles = step_index[0].astype(jnp.float32) * freqs
    timing = jnp.concatenate([jnp.cos(angles), jnp.sin(angles)]).astype(jnp.bfloat16)
    mod_share = jnp.dot(timing[None, :], mod_weight, preferred_element_type=jnp.float32)[0]
    modulation = lax.all_gather(
        lax.all_gather(mod_share, "ctx", axis=0, tiled=True), "head", axis=0, tiled=True
    )
    n_head = lax.axis_size("head")
    n_ctx = lax.axis_size("ctx")
    h_idx = lax.axis_index("head")
    c_idx = lax.axis_index("ctx")
    quarter = D // n_head
    scale = lax.dynamic_slice_in_dim(modulation, h_idx * quarter, quarter)
    shift = lax.dynamic_slice_in_dim(modulation, D + h_idx * quarter, quarter)
    weight_quarter = lax.all_gather(patch_weight, "ctx", axis=1, tiled=True)
    block_patches = lax.all_gather(patches, "head", axis=0, tiled=True)
    embedded = jnp.dot(block_patches, weight_quarter, preferred_element_type=jnp.float32)
    squares = lax.all_gather(jnp.sum(embedded * embedded, -1), "head", axis=0, tiled=False)
    inverse = lax.rsqrt(jnp.sum(squares, 0) / D + 1e-06)[:, None]
    normed_quarter = (embedded * inverse * (1.0 + scale) + shift).astype(jnp.bfloat16)
    normed = lax.all_gather(normed_quarter, "head", axis=1, tiled=True)
    group_rows = normed.shape[0]
    heads_here = qkv_weight.shape[1]
    out_cols = heads_here * 3 * HDIM
    local = qkv_weight.reshape(qkv_weight.shape[0], out_cols)
    rows = local.shape[0]
    half_rows = rows // 2
    core = lax.axis_index("dp") % 2
    mine = lax.dynamic_slice_in_dim(local, core * half_rows, half_rows, 0)
    fetched = jnp.stack(
        [
            lax.ppermute(mine, "ctx", [(i, (i + s) % n_ctx) for i in range(n_ctx)])
            for s in range(1, n_ctx)
        ]
    )
    n_dp = lax.axis_size("dp")
    partner = lax.ppermute(fetched, "dp", [(i, i ^ 1) for i in range(n_dp)])
    weight = jnp.concatenate(
        [local, fetched.reshape(-1, out_cols), partner.reshape(-1, out_cols)], 0
    )
    pieces = [lax.dynamic_slice_in_dim(normed, c_idx * rows, rows, 1)]
    for side in (core, 1 - core):
        for s in range(1, n_ctx):
            block = (c_idx + n_ctx - s) % n_ctx
            pieces.append(
                lax.dynamic_slice_in_dim(normed, block * rows + side * half_rows, half_rows, 1)
            )
    qkv = jnp.dot(jnp.concatenate(pieces, 1), weight, preferred_element_type=jnp.float32)
    qkv = qkv.astype(jnp.bfloat16).reshape(group_rows, heads_here, 3, HDIM)
    query = qkv[:, :, 0]
    keys = qkv[:, :, 1]
    values = qkv[:, :, 2]
    inv_root = 1.0 / jnp.sqrt(jnp.float32(HDIM))
    best = jnp.full((heads_here, group_rows), -1e30, jnp.float32)
    key_piece = lax.all_gather(keys, "ctx", axis=0, tiled=True)
    value_piece = lax.all_gather(values, "ctx", axis=0, tiled=True)
    scores = (
        jnp.einsum("qhd,khd->hqk", query, key_piece, preferred_element_type=jnp.float32) * inv_root
    )
    new_best = jnp.maximum(best, jnp.max(scores, -1))
    probs = jnp.exp(scores - new_best[..., None])
    denom = jnp.sum(probs, -1)
    accum = jnp.einsum(
        "hqk,khd->hqd", probs.astype(jnp.bfloat16), value_piece, preferred_element_type=jnp.float32
    )
    best, denom, accum = (new_best, denom, accum)
    result = (accum / denom[..., None]).astype(jnp.bfloat16)
    return result.transpose(1, 0, 2).reshape(group_rows, heads_here * HDIM)


def solution(mesh):
    return jax.shard_map(
        shards,
        mesh=mesh,
        in_specs=(
            P("dp", "head", "ctx"),
            P("dp", "head", "ctx"),
            P(),
            P(),
            P(),
            P(None, ("head", "ctx")),
            P("dp"),
            P(None, ("head", "ctx")),
            P("ctx", "head", None, None),
        ),
        out_specs=P(("dp", "ctx"), "head"),
        check_vma=False,
    )
```

profile of v0, /device:TPU:1, one launch (start us, length us, event | category | flops | bytes accessed | tf_op | source)
XLA Modules:
  0.0 616.5 jit_solution(10998383300142862645)
XLA Ops:
  6.5 3.9 copy.39
  10.5 1.8 constant_dynamic-slice_fusion
  12.3 2.6 copy.40
  14.8 2.1 collective-permute-start.4
  17.0 1.6 collective-permute-start.5
  18.6 2.6 collective-permute-start.6
  23.1 1.7 reshape.52
  24.8 1.5 fusion.129
  26.3 3.7 collective-permute-start
  34.5 89.0 %all-reduce = f32[2560]{0:T(1024)} all-reduce(f32[2560]{0:T(1024)S(1)} %dynamic-update-slice), channel_id=1, replica_groups=mesh['dp'=4,'head'=4,'ctx'=8] {'ctx'}, use_global_device_ids=true, to_apply=%add | all-reduce | flops 2560 | bytes 20480
  124.2 10.9 %all-gather.4 = f32[4,1,2560]{2,1,0:T(1,128)} all-gather(f32[1,1,2560]{2,1,0:T(1,128)S(1)} %reshape.69), channel_id=1, replica_groups=mesh['dp'=4,'head'=4,'ctx'=8] {'head'}, dimensions={0}, use_global_device_ids=true | all-gather | bytes 51200 | tf_op jit(solution)/shard_map/all_gather | solution.py:82
  135.9 2.3 slice.243
  138.2 2.4 slice.218
  140.6 2.3 slice.231
  145.5 2.4 collective-permute-done.1
  148.0 1.3 collective-permute-start.2
  151.9 1.9 fusion.90
  153.8 2.0 collective-permute-done.3
  155.8 3.2 collective-permute-start.8
  159.0 2.1 fusion.82
  168.7 3.4 multiply_convert_fusion
  172.2 2.4 reshape.53
  174.5 3.1 copy.66
  177.6 3.6 reshape.54
  184.7 10.6 %all_gather.27 = bf16[512,768]{1,0:T(8,128)(2,1)S(1)} all-gather(bf16[128,768]{1,0:T(8,128)(2,1)} %reshape.55), channel_id=1, replica_groups=mesh['dp'=4,'head'=4,'ctx'=8] {'head'}, dimensions={0}, use_global_device_ids=true | all-gather | bytes 983040 | tf_op jit(solution)/shard_map/all_gather | solution.py:93
  195.3 1.4 collective-permute-start.9
  196.7 2.4 bitcast_dynamic-update-slice_fusion.6
  199.8 2.4 bitcast_dynamic-update-slice_fusion.5
  202.3 2.4 bitcast_dynamic-update-slice_fusion.4
  204.7 2.5 bitcast_dynamic-update-slice_fusion.3
  207.2 2.4 bitcast_dynamic-update-slice_fusion.2
  209.6 1.5 collective-permute-done.9
  212.3 2.7 collective-permute-done.10
  216.1 20.7 %collective-permute-start.11 = (bf16[7,320,1920]{2,1,0:T(8,128)(2,1)}, bf16[7,320,1920]{2,1,0:T(8,128)(2,1)}, u32[]{:S(2)}, u32[]{:S(2)}) collective-permute-start(bf16[7,320,1920]{2,1,0:T(8,128)(2,1)} %bitcast_dynamic-update-slice_fusion), channel_id=1, source_target_pairs={{0,32},{32,0},{64,96},{96,64},{1,33},{33,1},{65,97},{97,65},{2,34}... | collective-permute-start | bytes 25804808 | tf_op jit(solution)/shard_map/ppermute | solution.py:114
  236.8 4.2 multiply_reduce_fusion.1
  241.0 8.1 %all-gather.3 = f32[4,1,512]{2,1,0:T(1,128)S(1)} all-gather(f32[1,1,512]{2,1,0:T(1,128)S(1)} %bitcast.133), channel_id=2, replica_groups=mesh['dp'=4,'head'=4,'ctx'=8] {'head'}, dimensions={0}, use_global_device_ids=true | all-gather | bytes 10240 | tf_op jit(solution)/shard_map/all_gather | solution.py:95
  249.1 3.2 add_convert_fusion
  252.6 3.2 copy.47
  255.8 71.6 %all-gather.12.cloned.1.call-done = bf16[512,5120]{1,0:T(8,128)(2,1)} async-done(((bf16[512,1280]{1,0:T(8,128)(2,1)}), bf16[512,5120]{1,0:T(8,128)(2,1)}) %all-gather.12.cloned.1.call-update) | async-done | bytes 5242896 | tf_op jit(solution)/shard_map/all_gather | solution.py:98
  328.6 8.0 %constant_dynamic-slice_fusion.1 = (bf16[512,320]{1,0:T(8,128)(2,1)S(1)}, bf16[512,320]{1,0:T(8,128)(2,1)S(1)}, bf16[512,320]{1,0:T(8,128)(2,1)S(1)}, bf16[512,3...) fusion(bf16[512,5120]{1,0:T(8,128)(2,1)} %all-gather.12.cloned., ...), kind=kLoop, calls=%fused_computation.165 | loop fusion | bytes 9175096 | tf_op jit(solution)/shard_map/dynamic_slice | solution.py:123
  336.6 9.1 %concatenate.94 = bf16[512,5120]{1,0:T(8,128)(2,1)} concatenate(bf16[512,640]{1,0:T(8,128)(2,1)S(1)} %constant_dynamic-slice_fusion.15, bf16[512,320]{1,0:T(8,128)(2,1)} %get-tuple-element.18, bf16[512,320]{1,0:T(8,128)(2,1)} %get-tuple-element.17, bf16[512,320]{1,0:T(8,128)(2,1)} %get-tuple-element.16, bf16[512,320]{1,0:T(8,128)(2,1)} %get-tuple-element.15, ...), dimensions={1} | concatenate | bytes 10485760 | tf_op jit(solution)/shard_map/concatenate | solution.py:125
  345.7 18.2 %fusion.13 = bf16[512,1920]{1,0:T(8,128)(2,1)} fusion(bf16[512,5120]{1,0:T(8,128)(2,1)} %concatenate.94, bf16[2240,1920]{1,0:T(8,128)(2,1)} %bitcast.42, bf16[2240,1920]{1,0:T(8,128)(2,1)} %bitcast.41, bf16[640,1920]{1,0:T(8,128)(2,1)} %copy.47), kind=kOutput, calls=%fused_computation.30 | convolution fusion | flops 10126295040 | bytes 26869760 | tf_op jit(solution)/shard_map/dot_general | solution.py:125
  363.9 2.7 copy.48
  369.2 110.1 %all-gather.14.cloned.1.call-done = bf16[4096,5,1,128]{3,0,1,2:T(8,128)(2,1)} async-done(((bf16[512,5,1,128]{3,0,1,2:T(8,128)(2,1)}), bf16[4096,5,1,128]{3,0,1,2:T(8,128)(2,1)}) %all-gather.14.cloned.1.call-update) | async-done | bytes 5242896 | tf_op jit(solution)/shard_map/all_gather | solution.py:132
  479.3 19.3 %multiply_reduce_fusion = (f32[5,512]{1,0:T(8,128)S(1)}, f32[5,512,4096]{2,1,0:T(8,128)}) fusion(bf16[4096,5,1,128]{3,0,1,2:T(8,128)(2,1)} %all-gather.14.cloned.1.call-done, bf16[512,5,3,128]{0,3,2,1:T(8,128)(2,1)S(1)} %bitcast.127), kind=kOutput, calls=%fused_computation.1 | convolution fusion | flops 2705323520 | bytes 47851520 | tf_op jit(solution)/shard_map/qhd,khd->hqk/dot_general | solution.py:135
  498.6 17.4 %fusion = f32[5,512]{1,0:T(8,128)S(1)} fusion(f32[5,512,4096]{2,1,0:T(8,128)} %get-tuple-element.61, f32[5,512]{1,0:T(8,128)S(1)} %broadcast_maximum_fusion), kind=kLoop, calls=%fused_computation.2 | loop fusion | flops 31454720 | bytes 41963520 | tf_op jit(solution)/shard_map/reduce_sum | solution.py:139
  516.0 75.3 %all-gather.16.cloned.1.call-done = bf16[4096,5,1,128]{0,3,1,2:T(8,128)(2,1)} async-done(((bf16[512,5,1,128]{0,3,1,2:T(8,128)(2,1)}), bf16[4096,5,1,128]{0,3,1,2:T(8,128)(2,1)}) %all-gather.16.cloned.1.call-update) | async-done | bytes 5242896 | tf_op jit(solution)/shard_map/all_gather | solution.py:133
  591.3 17.4 %divide_convert_fusion = bf16[512,5,128]{0,2,1:T(8,128)(2,1)S(1)} fusion(bf16[4096,5,1,128]{0,3,1,2:T(8,128)(2,1)} %all-gather.16.cloned.1.call-done, f32[5,512,4096]{2,1,0:T(8,128)} %get-tuple-element.61, f32[5,512]{1,0:T(8,128)S(1)} %broadcast_maximum_fusion, f32[512,5]{0,1:T(8,128)S(1)} %bitcast.131), kind=kOutput, calls=%fused_computation.90 | convolution fusion | flops 2716467200 | bytes 47861760 | tf_op jit(solution)/shard_map/hqk,khd->hqd/dot_general | solution.py:140
  (81 shorter events, 30.6 us)
Async XLA Ops:
  6.5 174.7 %copy-start = (bf16[768,192]{0,1:T(8,128)(2,1)S(1)}, bf16[768,192]{0,1:T(8,128)(2,1)}, u32[]{:S(2)}) copy-start(bf16[768,192]{0,1:T(8,128)(2,1)} %param.13) | copy-start | bytes 884740
  6.5 230.3 %all-gather.10.cloned.1.call-start = ((), (), s32[]{:S(2)}) async-start(), calls=%async_computation | async-start | bytes 2211840 | tf_op jit(solution)/shard_map/all_gather | solution.py:92
  10.5 11.6 %copy-start.6 = (bf16[2,16,3072]{2,1,0:T(8,128)(2,1)S(1)}, bf16[2,16,3072]{2,1,0:T(8,128)(2,1)}, u32[]{:S(2)}) copy-start(bf16[2,16,3072]{2,1,0:T(8,128)(2,1)} %param.10) | copy-start | bytes 589828
  14.8 180.5 %collective-permute-start.4 = (bf16[320,1920]{1,0:T(8,128)(2,1)}, bf16[320,1920]{1,0:T(8,128)(2,1)}, u32[]{:S(2)}, u32[]{:S(2)}) collective-permute-start(bf16[320,1920]{1,0:T(8,128)(2,1)} %copy.40), channel_id=1, source_target_pairs={{0,1},{1,2},{2,3},{3,4},{4,5},{5,6},{6,7},{7,0},{8,9},{9,10},{10,1... | collective-permute-start | bytes 3686408 | tf_op jit(solution)/shard_map/ppermute | solution.py:109
  17.0 182.2 %collective-permute-start.5 = (bf16[320,1920]{1,0:T(8,128)(2,1)}, bf16[320,1920]{1,0:T(8,128)(2,1)}, u32[]{:S(2)}, u32[]{:S(2)}) collective-permute-start(bf16[320,1920]{1,0:T(8,128)(2,1)} %copy.40), channel_id=1, source_target_pairs={{0,2},{1,3},{2,4},{3,5},{4,6},{5,7},{6,0},{7,1},{8,10},{9,11},{10,... | collective-permute-start | bytes 3686408 | tf_op jit(solution)/shard_map/ppermute | solution.py:109
  18.6 183.7 %collective-permute-start.6 = (bf16[320,1920]{1,0:T(8,128)(2,1)}, bf16[320,1920]{1,0:T(8,128)(2,1)}, u32[]{:S(2)}, u32[]{:S(2)}) collective-permute-start(bf16[320,1920]{1,0:T(8,128)(2,1)} %copy.40), channel_id=1, source_target_pairs={{0,3},{1,4},{2,5},{3,6},{4,7},{5,0},{6,1},{7,2},{8,11},{9,12},{10,... | collective-permute-start | bytes 3686408 | tf_op jit(solution)/shard_map/ppermute | solution.py:109
  21.2 183.5 %collective-permute-start.7 = (bf16[320,1920]{1,0:T(8,128)(2,1)}, bf16[320,1920]{1,0:T(8,128)(2,1)}, u32[]{:S(2)}, u32[]{:S(2)}) collective-permute-start(bf16[320,1920]{1,0:T(8,128)(2,1)} %copy.40), channel_id=1, source_target_pairs={{0,4},{1,5},{2,6},{3,7},{4,0},{5,1},{6,2},{7,3},{8,12},{9,13},{10,... | collective-permute-start | bytes 3686408 | tf_op jit(solution)/shard_map/ppermute | solution.py:109
  22.1 9.7 %copy-start.9 = (u32[128]{0:T(128)S(1)}, u32[128]{0:T(128)}, u32[]{:S(2)}) copy-start(u32[128]{0:T(128)} %constant.137) | copy-start | bytes 1540
  26.3 116.6 %collective-permute-start = (bf16[6,1,32,96]{3,2,1,0:T(8,128)(2,1)}, bf16[6,1,32,96]{3,2,1,0:T(8,128)(2,1)}, u32[]{:S(2)}, u32[]{:S(2)}) collective-permute-start(bf16[6,1,32,96]{3,2,1,0:T(8,128)(2,1)} %get-tuple-element.49), channel_id=1, source_target_pairs={{0,8},{8,16},{16,24},{1,9},{9,17},{17,25},{2,10},{10,18},{18,26},{... | collective-permute-start | bytes 110600 | tf_op jit(solution)/shard_map/ppermute | solution.py:19
  30.0 297.4 %all-gather.12.cloned.1.call-start = ((), (), s32[]{:S(2)}) async-start(), calls=%async_computation.1 | async-start | bytes 6553600 | tf_op jit(solution)/shard_map/all_gather | solution.py:98
  31.0 114.0 %copy-start.2 = (bf16[6,16,32,96]{3,2,1,0:T(8,128)(2,1)S(1)}, bf16[6,16,32,96]{3,2,1,0:T(8,128)(2,1)}, u32[]{:S(2)}) copy-start(bf16[6,16,32,96]{3,2,1,0:T(8,128)(2,1)} %reshape.52) | copy-start | bytes 1769476
  142.9 5.0 collective-permute-start.1
  148.0 2.5 collective-permute-start.2
  150.6 5.2 collective-permute-start.3
  153.8 7.3 %copy-start.7 = (bf16[3,3,288,192]{3,2,1,0:T(8,128)(2,1)S(1)}, bf16[3,3,288,192]{3,2,1,0:T(8,128)(2,1)}, u32[]{:S(2)}) copy-start(bf16[3,3,288,192]{3,2,1,0:T(8,128)(2,1)} %param.11) | copy-start | bytes 2985988
  155.8 51.4 %collective-permute-start.8 = (bf16[320,1920]{1,0:T(8,128)(2,1)}, bf16[320,1920]{1,0:T(8,128)(2,1)}, u32[]{:S(2)}, u32[]{:S(2)}) collective-permute-start(bf16[320,1920]{1,0:T(8,128)(2,1)} %copy.40), channel_id=1, source_target_pairs={{0,5},{1,6},{2,7},{3,0},{4,1},{5,2},{6,3},{7,4},{8,13},{9,14},{10,... | collective-permute-start | bytes 3686408 | tf_op jit(solution)/shard_map/ppermute | solution.py:109
  164.7 1.0 copy-start.5
  165.7 1.0 copy-start.4
  166.8 1.0 copy-start.3
  167.8 0.9 copy-start.8
  195.3 15.8 %collective-permute-start.9 = (bf16[320,1920]{1,0:T(8,128)(2,1)}, bf16[320,1920]{1,0:T(8,128)(2,1)S(1)}, u32[]{:S(2)}, u32[]{:S(2)}) collective-permute-start(bf16[320,1920]{1,0:T(8,128)(2,1)} %copy.40), channel_id=1, source_target_pairs={{0,6},{1,7},{2,0},{3,1},{4,2},{5,3},{6,4},{7,5},{8,14},{9,15},{10,... | collective-permute-start | bytes 3686408 | tf_op jit(solution)/shard_map/ppermute | solution.py:109
  199.1 15.8 %collective-permute-start.10 = (bf16[320,1920]{1,0:T(8,128)(2,1)}, bf16[320,1920]{1,0:T(8,128)(2,1)S(1)}, u32[]{:S(2)}, u32[]{:S(2)}) collective-permute-start(bf16[320,1920]{1,0:T(8,128)(2,1)} %copy.40), channel_id=1, source_target_pairs={{0,7},{1,0},{2,1},{3,2},{4,3},{5,4},{6,5},{7,6},{8,15},{9,8},{10,9... | collective-permute-start | bytes 3686408 | tf_op jit(solution)/shard_map/ppermute | solution.py:109
  216.1 129.6 %collective-permute-start.11 = (bf16[7,320,1920]{2,1,0:T(8,128)(2,1)}, bf16[7,320,1920]{2,1,0:T(8,128)(2,1)}, u32[]{:S(2)}, u32[]{:S(2)}) collective-permute-start(bf16[7,320,1920]{2,1,0:T(8,128)(2,1)} %bitcast_dynamic-update-slice_fusion), channel_id=1, source_target_pairs={{0,32},{32,0},{64,96},{96,64},{1,33},{33,1},{65,97},{97,65},{2,34}... | collective-permute-start | bytes 25804808 | tf_op jit(solution)/shard_map/ppermute | solution.py:114
  252.4 226.9 %all-gather.14.cloned.1.call-start = ((), (), s32[]{:S(2)}) async-start(), calls=%async_computation.2 | async-start | bytes 5898240 | tf_op jit(solution)/shard_map/all_gather | solution.py:132
  368.6 222.7 %all-gather.16.cloned.1.call-start = ((), (), s32[]{:S(2)}) async-start(), calls=%async_computation.3 | async-start | bytes 5898240 | tf_op jit(solution)/shard_map/all_gather | solution.py:133
  591.3 18.5 %copy-start.1 = (bf16[768,192]{0,1:T(8,128)(2,1)S(1)}, bf16[768,192]{0,1:T(8,128)(2,1)}, u32[]{:S(2)}) copy-start(bf16[768,192]{0,1:T(8,128)(2,1)} %param.13) | copy-start | bytes 884740
Sparse Core Ops, SparseCore 0:
  30.1 81.6 all-gather.9
  252.5 74.8 all-gather.11
  368.7 110.5 all-gather.13
  480.8 110.4 all-gather.15
where the time goes:
time: 625 us; the launch traced here: 617 us
  waiting for transfers between devices  267 us (43%)
  blocking collectives  119 us (19%)
  local copies, waits for them, and re-layouts  77.3 us (12%)
  matrix products  71.9 us (12%)
  starting transfers between devices  41 us (7%)
  other arithmetic  25.5 us (4%)
  between operations  15.2 us (2%)
    all_gather x1, waiting for transfers between devices, shards(): key_piece = lax.all_gather(keys, 'ctx', axis=0, tiled=True)  110 us
    unnamed x1, blocking collectives  89 us
    all_gather x1, waiting for transfers between devices, shards(): value_piece = lax.all_gather(values, 'ctx', axis=0, tiled=True)  75.3 us
    all_gather x1, waiting for transfers between devices, shards(): normed = lax.all_gather(normed_quarter, 'head', axis=1, tiled=True)  71.6 us
    unnamed x35, local copies, waits for them, and re-layouts  21.6 us
    ppermute x1, starting transfers between devices, shards(): partner = lax.ppermute(fetched, 'dp', [(i, i ^ 1) for i in range(n_dp)])  20.7 us
    dot_general x1, matrix products, shards(): jnp.einsum('qhd,khd->hqk', query, key_piece, preferred_element_type=jnp.f...  19.3 us
    dot_general x1, matrix products, shards(): jnp.dot(jnp.concatenate(pieces, 1), weight, preferred_element_type=jnp.fl...  18.2 us
  transfers between devices with their start and end apart: 16, of which 8 were waited for; matrix products, arithmetic and copies ran while one was open for 20% of the time, Pallas kernels for 0%

commit v1 on v0

--- a/solution.py
+++ b/solution.py
@@ -129,8 +129,12 @@
     values = qkv[:, :, 2]
     inv_root = 1.0 / jnp.sqrt(jnp.float32(HDIM))
     best = jnp.full((heads_here, group_rows), -1e30, jnp.float32)
-    key_piece = lax.all_gather(keys, "ctx", axis=0, tiled=True)
-    value_piece = lax.all_gather(values, "ctx", axis=0, tiled=True)
+    place_record = lambda inp, raw, row_axis: jnp.split(
+        lax.all_gather(jnp.concatenate([inp, raw], 1), row_axis, axis=0, tiled=True),
+        [inp.shape[1]],
+        1,
+    )
+    key_piece, value_piece = place_record(keys, raw=values, row_axis="ctx")
     scores = (
         jnp.einsum("qhd,khd->hqk", query, key_piece, preferred_element_type=jnp.float32) * inv_root
     )

time: 625 us -> 664 us (1.062)
  waiting for transfers between devices: 267 us -> 296 us
  blocking collectives: 119 us -> 127 us
    all_gather x2 -> x1, waiting for transfers between devices: 185 us -> 208 us  [shards(): lax.all_gather(jnp.concatenate([inp, raw], 1), row_axis, axis=0, tiled=True)]
    unnamed x1, blocking collectives: 89 us -> 97.6 us
    unnamed x35 -> x36, local copies, waits for them, and re-layouts: 21.6 us -> 21.6 us
  transfers between devices with their start and end apart: 16 -> 15, of which waited for: 8 -> 6; matrix products, arithmetic and copies ran while one was open for 20% -> 13% of each run, Pallas kernels for 0% -> 0%
where the time goes in v1:
time: 664 us; the launch traced here: 655 us
  waiting for transfers between devices  296 us (45%)
  blocking collectives  127 us (19%)
  local copies, waits for them, and re-layouts  78.2 us (12%)
  matrix products  71.7 us (11%)
  starting transfers between devices  39.1 us (6%)
  other arithmetic  28 us (4%)
  between operations  15.3 us (2%)
    all_gather x1, waiting for transfers between devices, shards(): lax.all_gather(jnp.concatenate([inp, raw], 1), row_axis, axis=0, tiled=True)  208 us
    unnamed x1, blocking collectives  97.6 us
    all_gather x1, waiting for transfers between devices, shards(): normed = lax.all_gather(normed_quarter, 'head', axis=1, tiled=True)  73.6 us
    unnamed x36, local copies, waits for them, and re-layouts  21.6 us
    ppermute x1, starting transfers between devices, shards(): partner = lax.ppermute(fetched, 'dp', [(i, i ^ 1) for i in range(n_dp)])  19.3 us
    dot_general x1, matrix products, shards(): jnp.einsum('qhd,khd->hqk', query, key_piece, preferred_element_type=jnp.f...  18.8 us
    dot_general x1, matrix products, shards(): jnp.dot(jnp.concatenate(pieces, 1), weight, preferred_element_type=jnp.fl...  18.1 us
    dot_general x1, matrix products, shards(): jnp.einsum('hqk,khd->hqd', probs.astype(jnp.bfloat16), value_piece, prefe...  17.8 us
  transfers between devices with their start and end apart: 15, of which 6 were waited for; matrix products, arithmetic and copies ran while one was open for 13% of the time, Pallas kernels for 0%

profile of v1, /device:TPU:1, one launch (start us, length us, event | category | flops | bytes accessed | tf_op | source)
XLA Modules:
  0.0 655.1 jit_solution(9029111414461637670)
XLA Ops:
  6.5 3.9 copy.42
  10.5 1.8 constant_dynamic-slice_fusion
  12.3 2.5 copy.43
  14.8 5.6 collective-permute-start.10
  20.5 1.3 collective-permute-start.5
  23.0 1.7 reshape.52
  24.7 1.5 fusion.129
  26.1 3.7 collective-permute-start
  34.3 97.6 %all-reduce = f32[2560]{0:T(1024)} all-reduce(f32[2560]{0:T(1024)S(1)} %dynamic-update-slice), channel_id=1, replica_groups=mesh['dp'=4,'head'=4,'ctx'=8] {'ctx'}, use_global_device_ids=true, to_apply=%add | all-reduce | flops 2560 | bytes 20480
  132.5 10.2 %all-gather.2 = f32[4,1,2560]{2,1,0:T(1,128)} all-gather(f32[1,1,2560]{2,1,0:T(1,128)S(1)} %reshape.67), channel_id=1, replica_groups=mesh['dp'=4,'head'=4,'ctx'=8] {'head'}, dimensions={0}, use_global_device_ids=true | all-gather | bytes 51200 | tf_op jit(solution)/shard_map/all_gather | solution.py:82
  143.6 2.3 slice.243
  145.9 2.3 slice.218
  148.2 2.3 slice.231
  153.1 2.4 collective-permute-done.1
  155.7 1.3 collective-permute-start.3
  157.5 3.1 collective-permute-done.3
  160.6 1.6 collective-permute-start.2
  162.2 2.2 fusion.82
  165.7 1.9 fusion.90
  175.1 3.4 multiply_convert_fusion
  178.5 2.4 reshape.53
  180.9 3.1 copy.71
  183.9 3.2 reshape.54
  190.6 11.0 %all_gather.24 = bf16[512,768]{1,0:T(8,128)(2,1)S(1)} all-gather(bf16[128,768]{1,0:T(8,128)(2,1)} %reshape.55), channel_id=1, replica_groups=mesh['dp'=4,'head'=4,'ctx'=8] {'head'}, dimensions={0}, use_global_device_ids=true | all-gather | bytes 983040 | tf_op jit(solution)/shard_map/all_gather | solution.py:93
  202.9 2.4 bitcast_dynamic-update-slice_fusion.6
  205.3 2.3 collective-permute-start.8
  207.7 2.4 bitcast_dynamic-update-slice_fusion.5
  210.1 2.4 bitcast_dynamic-update-slice_fusion.4
  212.5 6.5 collective-permute-done.7
  220.2 2.0 collective-permute-done.8
  223.3 2.5 bitcast_dynamic-update-slice_fusion.1
  225.7 2.4 bitcast_dynamic-update-slice_fusion
  228.1 19.3 %collective-permute-start.11 = (bf16[7,320,1920]{2,1,0:T(8,128)(2,1)}, bf16[7,320,1920]{2,1,0:T(8,128)(2,1)}, u32[]{:S(2)}, u32[]{:S(2)}) collective-permute-start(bf16[7,320,1920]{2,1,0:T(8,128)(2,1)} %bitcast_dynamic-update-slice_fusion), channel_id=1, source_target_pairs={{0,32},{32,0},{64,96},{96,64},{1,33},{33,1},{65,97},{97,65},{2,34}... | collective-permute-start | bytes 25804808 | tf_op jit(solution)/shard_map/ppermute | solution.py:114
  247.4 4.2 multiply_reduce_fusion.1
  251.7 8.1 %all-gather.1 = f32[4,1,512]{2,1,0:T(1,128)S(1)} all-gather(f32[1,1,512]{2,1,0:T(1,128)S(1)} %bitcast.123), channel_id=2, replica_groups=mesh['dp'=4,'head'=4,'ctx'=8] {'head'}, dimensions={0}, use_global_device_ids=true | all-gather | bytes 10240 | tf_op jit(solution)/shard_map/all_gather | solution.py:95
  259.8 3.3 add_convert_fusion
  263.3 3.3 copy.50
  266.5 73.6 %all-gather.9.cloned.1.call-done = bf16[512,5120]{1,0:T(8,128)(2,1)} async-done(((bf16[512,1280]{1,0:T(8,128)(2,1)}), bf16[512,5120]{1,0:T(8,128)(2,1)}) %all-gather.9.cloned.1.call-update) | async-done | bytes 5242896 | tf_op jit(solution)/shard_map/all_gather | solution.py:98
  341.2 8.0 %constant_dynamic-slice_fusion.1 = (bf16[512,320]{1,0:T(8,128)(2,1)S(1)}, bf16[512,320]{1,0:T(8,128)(2,1)S(1)}, bf16[512,320]{1,0:T(8,128)(2,1)S(1)}, bf16[512,3...) fusion(bf16[512,5120]{1,0:T(8,128)(2,1)} %all-gather.9.cloned.1, ...), kind=kLoop, calls=%fused_computation.165 | loop fusion | bytes 9175096 | tf_op jit(solution)/shard_map/dynamic_slice | solution.py:123
  349.2 9.0 %concatenate.97 = bf16[512,5120]{1,0:T(8,128)(2,1)} concatenate(bf16[512,640]{1,0:T(8,128)(2,1)S(1)} %constant_dynamic-slice_fusion.15, bf16[512,320]{1,0:T(8,128)(2,1)} %get-tuple-element.18, bf16[512,320]{1,0:T(8,128)(2,1)} %get-tuple-element.17, bf16[512,320]{1,0:T(8,128)(2,1)} %get-tuple-element.16, bf16[512,320]{1,0:T(8,128)(2,1)} %get-tuple-element.15, ...), dimensions={1} | concatenate | bytes 10485760 | tf_op jit(solution)/shard_map/concatenate | solution.py:125
  358.3 18.1 %fusion.13 = bf16[512,1920]{1,0:T(8,128)(2,1)} fusion(bf16[512,5120]{1,0:T(8,128)(2,1)} %concatenate.97, bf16[2240,1920]{1,0:T(8,128)(2,1)} %bitcast.42, bf16[2240,1920]{1,0:T(8,128)(2,1)} %bitcast.41, bf16[640,1920]{1,0:T(8,128)(2,1)} %copy.50), kind=kOutput, calls=%fused_computation.30 | convolution fusion | flops 10126295040 | bytes 26869760 | tf_op jit(solution)/shard_map/dot_general | solution.py:125
  376.4 2.7 copy.51
  380.0 1.4 copy.68
  382.5 2.3 pad_maximum_fusion.2
  384.8 208.4 %all-gather.11.cloned.1.call-done = bf16[4096,10,128]{2,0,1:T(8,128)(2,1)} async-done(((bf16[512,10,128]{2,0,1:T(8,128)(2,1)}), bf16[4096,10,128]{2,0,1:T(8,128)(2,1)}) %all-gather.11.cloned.1.call-update) | async-done | bytes 10485776 | tf_op jit(solution)/shard_map/all_gather | solution.py:133
  593.2 18.8 %multiply_reduce_fusion = (f32[5,512]{1,0:T(8,128)S(1)}, f32[5,512,4096]{2,1,0:T(8,128)}) fusion(bf16[4096,10,128]{2,0,1:T(8,128)(2,1)} %all-gather.11.cloned.1.call-done, bf16[512,5,3,128]{0,3,2,1:T(8,128)(2,1)S(1)} %bitcast.115), kind=kOutput, calls=%fused_computation.1 | convolution fusion | flops 2705323520 | bytes 47851520 | tf_op jit(solution)/shard_map/qhd,khd->hqk/dot_general | solution.py:139
  611.9 17.5 %fusion = f32[5,512]{1,0:T(8,128)S(1)} fusion(f32[5,512,4096]{2,1,0:T(8,128)} %get-tuple-element.61, f32[5,512]{1,0:T(8,128)S(1)} %broadcast_maximum_fusion), kind=kLoop, calls=%fused_computation.2 | loop fusion | flops 31454720 | bytes 41963520 | tf_op jit(solution)/shard_map/reduce_sum | solution.py:143
  629.5 17.8 %divide_convert_fusion = bf16[512,5,128]{0,2,1:T(8,128)(2,1)S(1)} fusion(bf16[4096,10,128]{2,0,1:T(8,128)(2,1)} %all-gather.11.cloned.1.call-done, f32[5,512,4096]{2,1,0:T(8,128)} %get-tuple-element.61, f32[5,512]{1,0:T(8,128)S(1)} %broadcast_maximum_fusion, f32[512,5]{0,1:T(8,128)S(1)} %bitcast.122), kind=kOutput, calls=%fused_computation.91 | convolution fusion | flops 2716467200 | bytes 47861760 | tf_op jit(solution)/shard_map/hqk,khd->hqd/dot_general | solution.py:144
  (80 shorter events, 29.0 us)
Async XLA Ops:
  6.5 180.6 %copy-start = (bf16[768,192]{0,1:T(8,128)(2,1)S(1)}, bf16[768,192]{0,1:T(8,128)(2,1)}, u32[]{:S(2)}) copy-start(bf16[768,192]{0,1:T(8,128)(2,1)} %param.13) | copy-start | bytes 884740
  6.5 240.9 %all-gather.7.cloned.1.call-start = ((), (), s32[]{:S(2)}) async-start(), calls=%async_computation | async-start | bytes 2211840 | tf_op jit(solution)/shard_map/all_gather | solution.py:92
  12.2 9.7 %copy-start.6 = (bf16[2,16,3072]{2,1,0:T(8,128)(2,1)S(1)}, bf16[2,16,3072]{2,1,0:T(8,128)(2,1)}, u32[]{:S(2)}) copy-start(bf16[2,16,3072]{2,1,0:T(8,128)(2,1)} %param.10) | copy-start | bytes 589828
  14.8 210.9 %collective-permute-start.10 = (bf16[320,1920]{1,0:T(8,128)(2,1)}, bf16[320,1920]{1,0:T(8,128)(2,1)}, u32[]{:S(2)}, u32[]{:S(2)}) collective-permute-start(bf16[320,1920]{1,0:T(8,128)(2,1)} %copy.43), channel_id=1, source_target_pairs={{0,7},{1,0},{2,1},{3,2},{4,3},{5,4},{6,5},{7,6},{8,15},{9,8},{10,9... | collective-permute-start | bytes 3686408 | tf_op jit(solution)/shard_map/ppermute | solution.py:109
  20.4 202.9 %collective-permute-start.9 = (bf16[320,1920]{1,0:T(8,128)(2,1)}, bf16[320,1920]{1,0:T(8,128)(2,1)}, u32[]{:S(2)}, u32[]{:S(2)}) collective-permute-start(bf16[320,1920]{1,0:T(8,128)(2,1)} %copy.43), channel_id=1, source_target_pairs={{0,6},{1,7},{2,0},{3,1},{4,2},{5,3},{6,4},{7,5},{8,14},{9,15},{10,... | collective-permute-start | bytes 3686408 | tf_op jit(solution)/shard_map/ppermute | solution.py:109
  20.5 189.6 %collective-permute-start.6 = (bf16[320,1920]{1,0:T(8,128)(2,1)}, bf16[320,1920]{1,0:T(8,128)(2,1)}, u32[]{:S(2)}, u32[]{:S(2)}) collective-permute-start(bf16[320,1920]{1,0:T(8,128)(2,1)} %copy.43), channel_id=1, source_target_pairs={{0,3},{1,4},{2,5},{3,6},{4,7},{5,0},{6,1},{7,2},{8,11},{9,12},{10,... | collective-permute-start | bytes 3686408 | tf_op jit(solution)/shard_map/ppermute | solution.py:109
  20.5 184.8 %collective-permute-start.5 = (bf16[320,1920]{1,0:T(8,128)(2,1)}, bf16[320,1920]{1,0:T(8,128)(2,1)}, u32[]{:S(2)}, u32[]{:S(2)}) collective-permute-start(bf16[320,1920]{1,0:T(8,128)(2,1)} %copy.43), channel_id=1, source_target_pairs={{0,2},{1,3},{2,4},{3,5},{4,6},{5,7},{6,0},{7,1},{8,10},{9,11},{10,... | collective-permute-start | bytes 3686408 | tf_op jit(solution)/shard_map/ppermute | solution.py:109
  21.9 9.7 %copy-start.9 = (u32[128]{0:T(128)S(1)}, u32[128]{0:T(128)}, u32[]{:S(2)}) copy-start(u32[128]{0:T(128)} %constant.137) | copy-start | bytes 1540
  21.9 318.2 %all-gather.9.cloned.1.call-start = ((), (), s32[]{:S(2)}) async-start(), calls=%async_computation.1 | async-start | bytes 6553600 | tf_op jit(solution)/shard_map/all_gather | solution.py:98
  26.1 124.4 %collective-permute-start = (bf16[6,1,32,96]{3,2,1,0:T(8,128)(2,1)}, bf16[6,1,32,96]{3,2,1,0:T(8,128)(2,1)}, u32[]{:S(2)}, u32[]{:S(2)}) collective-permute-start(bf16[6,1,32,96]{3,2,1,0:T(8,128)(2,1)} %get-tuple-element.49), channel_id=1, source_target_pairs={{0,8},{8,16},{16,24},{1,9},{9,17},{17,25},{2,10},{10,18},{18,26},{... | collective-permute-start | bytes 110600 | tf_op jit(solution)/shard_map/ppermute | solution.py:19
  30.8 121.8 %copy-start.2 = (bf16[6,16,32,96]{3,2,1,0:T(8,128)(2,1)S(1)}, bf16[6,16,32,96]{3,2,1,0:T(8,128)(2,1)}, u32[]{:S(2)}) copy-start(bf16[6,16,32,96]{3,2,1,0:T(8,128)(2,1)} %reshape.52) | copy-start | bytes 1769476
  150.5 5.0 collective-permute-start.1
  155.7 4.9 collective-permute-start.3
  160.6 3.9 collective-permute-start.2
  164.4 3.1 copy-start.5
  164.4 3.1 copy-start.7
  164.4 37.2 %collective-permute-start.4 = (bf16[320,1920]{1,0:T(8,128)(2,1)}, bf16[320,1920]{1,0:T(8,128)(2,1)}, u32[]{:S(2)}, u32[]{:S(2)}) collective-permute-start(bf16[320,1920]{1,0:T(8,128)(2,1)} %copy.43), channel_id=1, source_target_pairs={{0,1},{1,2},{2,3},{3,4},{4,5},{5,6},{6,7},{7,0},{8,9},{9,10},{10,1... | collective-permute-start | bytes 3686408 | tf_op jit(solution)/shard_map/ppermute | solution.py:109
  170.3 1.0 copy-start.4
  173.1 1.0 copy-start.3
  174.1 0.9 copy-start.8
  201.7 17.3 %collective-permute-start.7 = (bf16[320,1920]{1,0:T(8,128)(2,1)}, bf16[320,1920]{1,0:T(8,128)(2,1)S(1)}, u32[]{:S(2)}, u32[]{:S(2)}) collective-permute-start(bf16[320,1920]{1,0:T(8,128)(2,1)} %copy.43), channel_id=1, source_target_pairs={{0,4},{1,5},{2,6},{3,7},{4,0},{5,1},{6,2},{7,3},{8,12},{9,13},{10,... | collective-permute-start | bytes 3686408 | tf_op jit(solution)/shard_map/ppermute | solution.py:109
  205.3 16.8 %collective-permute-start.8 = (bf16[320,1920]{1,0:T(8,128)(2,1)}, bf16[320,1920]{1,0:T(8,128)(2,1)S(1)}, u32[]{:S(2)}, u32[]{:S(2)}) collective-permute-start(bf16[320,1920]{1,0:T(8,128)(2,1)} %copy.43), channel_id=1, source_target_pairs={{0,5},{1,6},{2,7},{3,0},{4,1},{5,2},{6,3},{7,4},{8,13},{9,14},{10,... | collective-permute-start | bytes 3686408 | tf_op jit(solution)/shard_map/ppermute | solution.py:109
  228.1 130.1 %collective-permute-start.11 = (bf16[7,320,1920]{2,1,0:T(8,128)(2,1)}, bf16[7,320,1920]{2,1,0:T(8,128)(2,1)}, u32[]{:S(2)}, u32[]{:S(2)}) collective-permute-start(bf16[7,320,1920]{2,1,0:T(8,128)(2,1)} %bitcast_dynamic-update-slice_fusion), channel_id=1, source_target_pairs={{0,32},{32,0},{64,96},{96,64},{1,33},{33,1},{65,97},{97,65},{2,34}... | collective-permute-start | bytes 25804808 | tf_op jit(solution)/shard_map/ppermute | solution.py:114
  263.1 330.1 %all-gather.11.cloned.1.call-start = ((), (), s32[]{:S(2)}) async-start(), calls=%async_computation.2 | async-start | bytes 11796480 | tf_op jit(solution)/shard_map/all_gather | solution.py:133
  629.4 18.9 %copy-start.1 = (bf16[768,192]{0,1:T(8,128)(2,1)S(1)}, bf16[768,192]{0,1:T(8,128)(2,1)}, u32[]{:S(2)}) copy-start(bf16[768,192]{0,1:T(8,128)(2,1)} %param.13) | copy-start | bytes 884740
Sparse Core Ops, SparseCore 0:
  22.0 88.8 all-gather.6
  263.2 76.8 all-gather.8
  384.9 208.1 all-gather.10
